TPU v7x, 256 devices: a whole 4x4x8 slice. The times are simulated.
256 devices in a mesh: req: 32 (over x, y, core), tp: 8 (over z).
Axes of the slice: x: 4, y: 4, z: 8, core: 2. Of those that a mesh axis runs over, the one named last changes fastest.
Arguments:
- query: bfloat16 [768, 4096], P('req', 'tp'), may hold values from -102 to 102
- new_key: bfloat16 [768, 1024], P('req', 'tp'), may hold values from -6 to 6
- new_value: bfloat16 [768, 1024], P('req', 'tp'), may hold values from -6 to 6
- prefix_key: bfloat16 [64, 6144, 1024], P('req', None, 'tp'), may hold values from -6 to 6
- prefix_value: bfloat16 [64, 6144, 1024], P('req', None, 'tp'), may hold values from -6 to 6
- suffix_key: bfloat16 [768, 128, 1024], P('req', None, 'tp'), may hold values from -6 to 6
- suffix_value: bfloat16 [768, 128, 1024], P('req', None, 'tp'), may hold values from -6 to 6
- group_ids: int32 [768], replicated, may hold values from 0 to 63, as said below
- prompt_len: int32 [64], P('req'), may hold values from 768 to 6144, as said below
- suffix_len: int32 [768], replicated, may hold values from 1 to 128, as said below
- o_weight: bfloat16 [4096, 4096], P('tp'), may hold values from -0.09375 to 0.09375
- residual: bfloat16 [768, 4096], P('req'), may hold values from -0.29882812 to 0.29882812
- norm_gain: bfloat16 [4096], replicated, may hold values from 0.5 to 1.5
Outputs:
- hidden: bfloat16 [768, 4096], P('req')
- normed: bfloat16 [768, 4096], P('req')
Inputs may be any that keep to these rules, and one draw needn't show every extreme that they name: Request r belongs to group group_ids[r]; groups 2k to 2k + 1 at a time are held together (group // 2 names the holder). Among each aligned block of 24 requests, every holder that appears is named by exactly 2 of them. `prompt_len`: some group has exactly 6144. `suffix_len`: some request has exactly 128.
All inputs are finite; a program needn't handle non-finite values.
Results may differ from a plain program's by a relative error of at most 0.008.
Values may be sent and summed in bfloat16 or wider, within the bound.
No kernel may reach another device: no remote copies, remote signals or barrier semaphores. Data moves between devices by JAX's collectives and lax.ppermute only.
A program may use at most 64 MiB of HBM per device.

v0:
```python
import math
import jax
import jax.numpy as jnp
from jax import lax
from jax.sharding import PartitionSpec as P

HD = 128
WIN = 4096
SINKS = 4
FAR_BELOW = -1e30
NORM_EPS = 1e-06


def prefix_attend(
    rows_query, row_group, row_suffix, prefix_key, prefix_value, prompt_len, first_group, blocks
):
    row_count = rows_query.shape[0]
    groups_dev = prefix_key.shape[0]
    prompt_max = prefix_key.shape[1]
    kv_dev = prefix_key.shape[2] // HD
    heads_dev = rows_query.shape[1] // HD
    repeat = heads_dev // kv_dev
    block_len = min(512, prompt_max)
    score_scale = 1.0 / math.sqrt(HD)
    local_group = row_group - first_group
    owned = (local_group >= 0) & (local_group < groups_dev)
    member = local_group[:, None] == jnp.arange(groups_dev, dtype=jnp.int32)[None, :]
    row_prompt = jnp.sum(jnp.where(member, prompt_len[None, :], 0), axis=1)
    row_low = row_prompt + row_suffix - WIN + 1
    queries = rows_query.reshape(row_count, kv_dev, repeat, HD)

    def key_step(block_index, loop_state):
        running, weight_sum, weighted = loop_state
        key_start = block_index * block_len
        key_block = lax.dynamic_slice_in_dim(prefix_key, key_start, block_len, 1).reshape(
            groups_dev, block_len, kv_dev, HD
        )
        value_block = lax.dynamic_slice_in_dim(prefix_value, key_start, block_len, 1).reshape(
            groups_dev, block_len, kv_dev, HD
        )
        scores = (
            jnp.einsum("rkhd,gpkd->rkhgp", queries, key_block, preferred_element_type=jnp.float32)
            * score_scale
        )
        positions = key_start + jnp.arange(block_len, dtype=jnp.int32)
        inside = positions[None, :] < prompt_len[:, None]
        window = (positions[None, :] < SINKS) | (positions[None, :] >= row_low[:, None])
        usable = member[:, :, None] & inside[None, :, :] & window[:, None, :]
        usable = usable[:, None, None, :, :]
        masked = jnp.where(usable, scores, FAR_BELOW)
        updated = jnp.maximum(running, jnp.max(masked, axis=(3, 4)))
        weights = jnp.where(usable, jnp.exp(masked - updated[..., None, None]), 0.0)
        rescale = jnp.exp(running - updated)
        weight_sum = weight_sum * rescale + jnp.sum(weights, axis=(3, 4))
        rounded = weights.astype(jnp.bfloat16)
        weighted = weighted * rescale[..., None] + jnp.einsum(
            "rkhgp,gpkd->rkhd", rounded, value_block, preferred_element_type=jnp.float32
        )
        return (updated, weight_sum, weighted)

    initial = (
        jnp.full((row_count, kv_dev, repeat), FAR_BELOW, jnp.float32),
        jnp.zeros((row_count, kv_dev, repeat), jnp.float32),
        jnp.zeros((row_count, kv_dev, repeat, HD), jnp.float32),
    )
    running, weight_sum, weighted = lax.fori_loop(0, blocks, key_step, initial)
    bounded = jnp.maximum(weight_sum, 1.0)
    normalized = jnp.where(owned[:, None, None, None], weighted / bounded[..., None], 0.0).reshape(
        row_count, heads_dev * HD
    )
    log_total = jnp.where(owned[:, None, None], running + jnp.log(bounded), 0.0).reshape(
        row_count, heads_dev
    )
    return (normalized, log_total)


def body(
    query,
    new_key,
    new_value,
    prefix_key,
    prefix_value,
    suffix_key,
    suffix_value,
    group_ids,
    prompt_len,
    suffix_len,
    o_weight,
    residual,
    norm_gain,
):
    req_dev = query.shape[0]
    heads_dev = query.shape[1] // HD
    kv_dev = new_key.shape[1] // HD
    repeat = heads_dev // kv_dev
    groups_dev = prefix_key.shape[0]
    prompt_max = prefix_key.shape[1]
    suffix_max = suffix_key.shape[1]
    block_len = min(512, prompt_max)
    score_scale = 1.0 / math.sqrt(HD)
    places = lax.axis_size("req")
    device = lax.axis_index("req")
    first_group = device * groups_dev
    own_suffix = lax.dynamic_slice_in_dim(suffix_len, device * req_dev, req_dev)
    blocks = prompt_max // block_len
    capacity = max(2, req_dev // places)
    slot_total = places * capacity
    all_groups = group_ids.reshape(places, 1, req_dev)
    all_suffix = suffix_len.reshape(places, 1, req_dev)
    all_rows = (
        jnp.arange(places, dtype=jnp.int32)[:, None] * req_dev
        + jnp.arange(req_dev, dtype=jnp.int32)[None, :]
    ).reshape(places, 1, req_dev)
    is_mine = (group_ids // groups_dev).reshape(places, req_dev) == device
    slot_order = jnp.cumsum(is_mine.astype(jnp.int32), axis=1) - 1
    slot_pick = is_mine[:, None, :] & (
        slot_order[:, None, :] == jnp.arange(capacity, dtype=jnp.int32)[None, :, None]
    )
    filled = jnp.any(slot_pick, axis=2)
    slot_group = jnp.where(
        filled, jnp.sum(jnp.where(slot_pick, all_groups, 0), axis=2), -1
    ).reshape(slot_total)
    slot_suffix = jnp.sum(jnp.where(slot_pick, all_suffix, 0), axis=2).reshape(slot_total)
    slot_row = jnp.where(filled, jnp.sum(jnp.where(slot_pick, all_rows, 0), axis=2), -1).reshape(
        slot_total
    )
    every_query = lax.all_gather(query, "req", axis=0, tiled=True)
    pick_rows = slot_row[:, None] == jnp.arange(places * req_dev, dtype=jnp.int32)[None, :]
    compact = jnp.dot(
        pick_rows.astype(jnp.bfloat16), every_query, preferred_element_type=jnp.float32
    ).astype(jnp.bfloat16)
    part_out, part_log = prefix_attend(
        compact, slot_group, slot_suffix, prefix_key, prefix_value, prompt_len, first_group, blocks
    )
    spread_rows = pick_rows.T.astype(jnp.float32)
    spread_out = jnp.dot(spread_rows, part_out, precision=lax.Precision.HIGHEST)
    spread_log = jnp.dot(spread_rows, part_log, precision=lax.Precision.HIGHEST)
    prefix_out, prefix_log = (
        lax.psum_scatter(spread_out, "req", scatter_dimension=0, tiled=True),
        lax.psum_scatter(spread_log, "req", scatter_dimension=0, tiled=True),
    )
    queries = query.reshape(req_dev, kv_dev, repeat, HD)
    key_rows = suffix_key.reshape(req_dev, suffix_max, kv_dev, HD)
    value_rows = suffix_value.reshape(req_dev, suffix_max, kv_dev, HD)
    scores = (
        jnp.einsum("rkhd,rjkd->rkhj", queries, key_rows, preferred_element_type=jnp.float32)
        * score_scale
    )
    own_score = (
        jnp.einsum(
            "rkhd,rkd->rkh",
            queries,
            new_key.reshape(req_dev, kv_dev, HD),
            preferred_element_type=jnp.float32,
        )
        * score_scale
    )
    usable = (jnp.arange(suffix_max, dtype=jnp.int32)[None, :] < own_suffix[:, None])[
        :, None, None, :
    ]
    masked = jnp.where(usable, scores, FAR_BELOW)
    running = jnp.maximum(jnp.max(masked, axis=-1), own_score)
    weights = jnp.where(usable, jnp.exp(masked - running[..., None]), 0.0)
    own_weight = jnp.exp(own_score - running)
    weight_sum = jnp.sum(weights, axis=-1) + own_weight
    weighted = jnp.einsum(
        "rkhj,rjkd->rkhd",
        weights.astype(jnp.bfloat16),
        value_rows,
        preferred_element_type=jnp.float32,
    )
    own_rounded = own_weight.astype(jnp.bfloat16).astype(jnp.float32)
    weighted = weighted + own_rounded[..., None] * new_value.reshape(req_dev, kv_dev, 1, HD).astype(
        jnp.float32
    )
    local_out = weighted / weight_sum[..., None]
    local_log = running + jnp.log(weight_sum)
    prefix_out = prefix_out.reshape(req_dev, kv_dev, repeat, HD)
    prefix_log = prefix_log.reshape(req_dev, kv_dev, repeat)
    combined = jnp.logaddexp(prefix_log, local_log)
    attended = (
        prefix_out * jnp.exp(prefix_log - combined)[..., None]
        + local_out * jnp.exp(local_log - combined)[..., None]
    )
    attended = attended.reshape(req_dev, heads_dev * HD).astype(jnp.bfloat16)
    partial_value = jnp.dot(attended, o_weight, preferred_element_type=jnp.float32)
    proj = lax.psum(partial_value, "tp")
    summed = residual.astype(jnp.float32) + proj
    hidden = summed.astype(jnp.bfloat16)
    inverse = lax.rsqrt(jnp.mean(summed * summed, axis=-1, keepdims=True) + NORM_EPS)
    normed = (summed * inverse * norm_gain.astype(jnp.float32)[None, :]).astype(jnp.bfloat16)
    return (hidden, normed)


def solution(mesh):
    placed = (
        P("req", "tp"),
        P("req", "tp"),
        P("req", "tp"),
        P("req", None, "tp"),
        P("req", None, "tp"),
        P("req", None, "tp"),
        P("req", None, "tp"),
        P(),
        P("req"),
        P(),
        P("tp", None),
        P("req", None),
        P(),
    )
    return jax.shard_map(
        body,
        mesh=mesh,
        in_specs=placed,
        out_specs=(P("req", None), P("req", None)),
        check_vma=False,
    )
```

profile of v0, /device:TPU:2, one launch (start us, length us, event | category | flops | bytes accessed | tf_op | source)
XLA Modules:
  0.0 305.6 jit_solution(10688126659396240701)
XLA Ops:
  11.4 24.9 %all_gather.3 = bf16[768,512]{1,0:T(8,128)(2,1)S(1)} all-gather(bf16[24,512]{1,0:T(8,128)(2,1)} %param.15), channel_id=1, replica_groups=mesh['req'=32,'tp'=8] {'req'}, dimensions={0}, use_global_device_ids=true | all-gather | bytes 811008 | tf_op jit(solution)/shard_map/all_gather | solution.py:127
  36.8 50.0 %while.18 = (s32[]{:T(128)}, f32[64,1,4]{0,2,1:T(4,128)S(1)}, f32[64,1,4]{0,2,1:T(4,128)S(1)}, f32[64,1,4,128]{3,0,2,1:T(8,128)S(1)}, s32[2]{0:T(128)}, /*index=...) while((s32[]{:T(128)}, f32[64,1,4]{0,2,1:T(4,128)S(1)}, ...), condition=%wide.region_9.10_spmd.clone, body=%wide.region_6.9_spmd.clone.sunk | while | flops 136876160 | bytes 4351967 | solution.py:66
  37.8 1.4 fusion.83
  39.6 1.4 fusion.86
  42.0 1.4 fusion.83
  43.8 1.4 fusion.86
  47.9 1.4 fusion.86
  52.1 1.4 fusion.86
  56.3 1.4 fusion.86
  58.7 1.4 fusion.83
  60.5 1.4 fusion.86
  62.9 1.4 fusion.83
  64.6 1.4 fusion.86
  68.8 1.4 fusion.86
  73.0 1.4 fusion.86
  77.1 1.4 fusion.86
  81.3 1.4 fusion.86
  83.7 1.4 fusion.83
  85.5 1.4 fusion.86
  87.2 2.0 fusion.27
  91.6 109.0 %all-reduce = f32[768,4]{0,1:T(4,128)S(1)} all-reduce(f32[768,4]{0,1:T(4,128)S(1)} %fusion.26), channel_id=3, replica_groups=mesh['req'=32,'tp'=8] {'req'}, use_global_device_ids=true, to_apply=%region_11.12.clone | all-reduce | flops 3072 | bytes 24576
  203.2 3.6 %fusion.37 = f32[24,4096]{1,0:T(8,128)} fusion(bf16[512,4096]{1,0:T(8,128)(2,1)} %param.25, bf16[3,8,4,128]{3,2,1,0:T(4,128)(2,1)S(1)} %bitcast.93), kind=kOutput, calls=%fused_computation.57 | convolution fusion | flops 100663296 | bytes 4612096 | tf_op jit(solution)/shard_map/dot_general | solution.py:186
  206.8 88.9 %all-reduce.3.cloned.1.call-done = f32[24,4096]{1,0:T(8,128)} async-done(((f32[24,4096]{1,0:T(8,128)}), f32[24,4096]{1,0:T(8,128)}) %all-reduce.3.cloned.1.call-update) | async-done | bytes 393232 | tf_op jit(solution)/shard_map/psum | solution.py:187
  297.0 1.8 multiply_convert_fusion
  (201 shorter events, 35.8 us)
Async XLA Ops:
  7.2 193.8 %copy-start = (bf16[24,128,128]{2,1,0:T(8,128)(2,1)S(1)}, bf16[24,128,128]{2,1,0:T(8,128)(2,1)}, u32[]{:S(2)}) copy-start(bf16[24,128,128]{2,1,0:T(8,128)(2,1)} %param.20) | copy-start | bytes 2359300
  7.2 194.8 %reduce-scatter.3.cloned.1.call-start = ((), (), s32[]{:S(2)}) async-start(), calls=%async_computation.1 | async-start | bytes 1622016 | tf_op jit(solution)/shard_map/reduce_scatter | solution.py:139
  86.9 2.4 copy-start.2
  86.9 3.2 %copy-start.7 = (u32[256]{0:T(256)S(1)}, u32[256]{0:T(256)}, u32[]{:S(2)}) copy-start(u32[256]{0:T(256)} %constant.130) | copy-start | bytes 3076
  86.9 113.9 %copy-start.4 = (bf16[24,128]{1,0:T(8,128)(2,1)S(1)}, bf16[24,128]{1,0:T(8,128)(2,1)}, u32[]{:S(2)}) copy-start(bf16[24,128]{1,0:T(8,128)(2,1)} %param.17) | copy-start | bytes 18436
  86.9 113.9 %copy-start.6 = (bf16[24,128]{1,0:T(8,128)(2,1)S(1)}, bf16[24,128]{1,0:T(8,128)(2,1)}, u32[]{:S(2)}) copy-start(bf16[24,128]{1,0:T(8,128)(2,1)} %param.16) | copy-start | bytes 18436
  86.9 115.8 %copy-start.5 = (bf16[24,128,128]{2,1,0:T(8,128)(2,1)S(1)}, bf16[24,128,128]{2,1,0:T(8,128)(2,1)}, u32[]{:S(2)}) copy-start(bf16[24,128,128]{2,1,0:T(8,128)(2,1)} %param.21) | copy-start | bytes 2359300
  89.2 206.5 %all-reduce.3.cloned.1.call-start = ((), (), s32[]{:S(2)}) async-start(), calls=%async_computation.2 | async-start | bytes 786432 | tf_op jit(solution)/shard_map/psum | solution.py:187
  202.8 4.0 %copy-start.3 = (bf16[4096]{0:T(1024)(128)(2,1)S(1)}, bf16[4096]{0:T(1024)(128)(2,1)}, u32[]{:S(2)}) copy-start(bf16[4096]{0:T(1024)(128)(2,1)} %param.27) | copy-start | bytes 24580
  202.8 93.0 %copy-start.1 = (bf16[24,4096]{1,0:T(8,128)(2,1)S(1)}, bf16[24,4096]{1,0:T(8,128)(2,1)}, u32[]{:S(2)}) copy-start(bf16[24,4096]{1,0:T(8,128)(2,1)} %param.26) | copy-start | bytes 589828
Sparse Core Ops, SparseCore 0:
  89.4 86.8 reduce-scatter.2
  206.9 88.8 all-reduce.2
where the time goes:
time: 307 us; the launch traced here: 306 us
  blocking collectives  134 us (44%)
  waiting for transfers between devices  89 us (29%)
  matrix products  40.4 us (13%)
  other arithmetic  21.3 us (7%)
  between operations  15 us (5%)
  local copies, waits for them, and re-layouts  5.04 us (2%)
    unnamed x1, blocking collectives  109 us
    psum x1, waiting for transfers between devices, body(): proj = lax.psum(partial_value, 'tp')  88.9 us
    all_gather x1, blocking collectives, body(): every_query = lax.all_gather(query, 'req', axis=0, tiled=True)  24.9 us
    dot_general x12, matrix products, key_step(): jnp.einsum('rkhgp,gpkd->rkhd', rounded, value_block, preferred_element_ty...  16.8 us
    dot_general x12, matrix products, key_step(): jnp.einsum('rkhd,gpkd->rkhgp', queries, key_block, preferred_element_type...  16.3 us
    lt x12, other arithmetic, key_step(): inside = positions[None, :] < prompt_len[:, None]  8.77 us
  transfers between devices with their start and end apart: 2, of which 1 were waited for; matrix products, arithmetic and copies ran while one was open for 1% of the time, Pallas kernels for 0%

commit v1 on v0

--- a/solution.py
+++ b/solution.py
@@ -184,7 +184,9 @@
     )
     attended = attended.reshape(req_dev, heads_dev * HD).astype(jnp.bfloat16)
     partial_value = jnp.dot(attended, o_weight, preferred_element_type=jnp.float32)
-    proj = lax.psum(partial_value, "tp")
+    proj = partial_value
+    for hop in (1, 2, 4):
+        proj = proj + lax.ppermute(proj, "tp", [(dev, dev ^ hop) for dev in range(8)])
     summed = residual.astype(jnp.float32) + proj
     hidden = summed.astype(jnp.bfloat16)
     inverse = lax.rsqrt(jnp.mean(summed * summed, axis=-1, keepdims=True) + NORM_EPS)

time: 307 us -> 280 us (0.912)
  the two profiles are of different devices: /device:TPU:2 before, /device:TPU:30 now
where the time goes in v1:
time: 280 us; the launch traced here: 278 us
  blocking collectives  143 us (51%)
  waiting for transfers between devices  42.4 us (15%)
  matrix products  39.6 us (14%)
  other arithmetic  19.3 us (7%)
  between operations  15 us (5%)
  starting transfers between devices  13.2 us (5%)
  local copies, waits for them, and re-layouts  5.03 us (2%)
    unnamed x1, blocking collectives  120 us
    ppermute x3, waiting for transfers between devices, body(): lax.ppermute(proj, 'tp', [(dev, dev ^ hop) for dev in range(8)])  42.4 us
    all_gather x1, blocking collectives, body(): every_query = lax.all_gather(query, 'req', axis=0, tiled=True)  22.6 us
    dot_general x12, matrix products, key_step(): jnp.einsum('rkhgp,gpkd->rkhd', rounded, value_block, preferred_element_ty...  16.8 us
    dot_general x12, matrix products, key_step(): jnp.einsum('rkhd,gpkd->rkhgp', queries, key_block, preferred_element_type...  16.2 us
    ppermute x3, starting transfers between devices, body(): lax.ppermute(proj, 'tp', [(dev, dev ^ hop) for dev in range(8)])  13.1 us
    lt x12, other arithmetic, key_step(): inside = positions[None, :] < prompt_len[:, None]  8.77 us
  transfers between devices with their start and end apart: 4, of which 3 were waited for; matrix products, arithmetic and copies ran while one was open for 1% of the time, Pallas kernels for 0%

profile of v1, /device:TPU:30, one launch (start us, length us, event | category | flops | bytes accessed | tf_op | source)
XLA Modules:
  0.0 278.4 jit_solution(9452365454660945509)
XLA Ops:
  11.4 22.6 %all_gather.3 = bf16[768,512]{1,0:T(8,128)(2,1)S(1)} all-gather(bf16[24,512]{1,0:T(8,128)(2,1)} %param.15), channel_id=1, replica_groups=mesh['req'=32,'tp'=8] {'req'}, dimensions={0}, use_global_device_ids=true | all-gather | bytes 811008 | tf_op jit(solution)/shard_map/all_gather | solution.py:127
  34.6 50.0 %while.18 = (s32[]{:T(128)}, f32[64,1,4]{0,2,1:T(4,128)S(1)}, f32[64,1,4]{0,2,1:T(4,128)S(1)}, f32[64,1,4,128]{3,0,2,1:T(8,128)S(1)}, s32[2]{0:T(128)}, /*index=...) while((s32[]{:T(128)}, f32[64,1,4]{0,2,1:T(4,128)S(1)}, ...), condition=%wide.region_9.10_spmd.clone, body=%wide.region_6.9_spmd.clone.sunk | while | flops 136876160 | bytes 4351967 | solution.py:66
  37.4 1.4 fusion.85
  41.5 1.4 fusion.85
  43.9 1.4 fusion.82
  45.7 1.4 fusion.85
  49.9 1.4 fusion.85
  54.0 1.4 fusion.85
  58.2 1.4 fusion.85
  62.4 1.4 fusion.85
  66.5 1.4 fusion.85
  70.7 1.4 fusion.85
  74.8 1.4 fusion.85
  79.0 1.4 fusion.85
  83.2 1.4 fusion.85
  84.9 2.0 fusion.27
  89.2 120.3 %all-reduce = f32[768,4]{0,1:T(4,128)S(1)} all-reduce(f32[768,4]{0,1:T(4,128)S(1)} %fusion.26), channel_id=3, replica_groups=mesh['req'=32,'tp'=8] {'req'}, use_global_device_ids=true, to_apply=%region_11.12.clone | all-reduce | flops 3072 | bytes 24576
  212.0 2.9 %fusion.36 = f32[24,4096]{1,0:T(8,128)S(1)} fusion(bf16[512,4096]{1,0:T(8,128)(2,1)} %param.25, bf16[3,8,4,128]{3,2,1,0:T(4,128)(2,1)S(1)} %bitcast.93), kind=kOutput, calls=%fused_computation.56 | convolution fusion | flops 100663296 | bytes 4612096 | tf_op jit(solution)/shard_map/dot_general | solution.py:186
  214.9 1.9 collective-permute-start
  216.9 7.5 %collective-permute-done = f32[24,4096]{1,0:T(8,128)S(1)} collective-permute-done((f32[24,4096]{1,0:T(8,128)S(1)}, f32[24,4096]{1,0:T(8,128)S(1)}, u32[]{:S(2)}, u32[]{:S(2)}) %collective-permute-start) | collective-permute-done | bytes 393248 | tf_op jit(solution)/shard_map/ppermute | solution.py:189
  224.4 3.4 %collective-permute-start.1 = (f32[24,4096]{1,0:T(8,128)S(1)}, f32[24,4096]{1,0:T(8,128)S(1)}, u32[]{:S(2)}, u32[]{:S(2)}) collective-permute-start(f32[24,4096]{1,0:T(8,128)S(1)} %add.162), channel_id=1, source_target_pairs={{0,2},{1,3},{2,0},{3,1},{4,6},{5,7},{6,4},{7,5},{8,10},{9,11},{10,... | collective-permute-start | bytes 1179656 | tf_op jit(solution)/shard_map/ppermute | solution.py:189
  227.8 17.0 %collective-permute-done.1 = f32[24,4096]{1,0:T(8,128)S(1)} collective-permute-done((f32[24,4096]{1,0:T(8,128)S(1)}, f32[24,4096]{1,0:T(8,128)S(1)}, u32[]{:S(2)}, u32[]{:S(2)}) %collective-permute-start.1) | collective-permute-done | bytes 393248 | tf_op jit(solution)/shard_map/ppermute | solution.py:189
  244.8 7.8 %collective-permute-start.2 = (f32[24,4096]{1,0:T(8,128)S(1)}, f32[24,4096]{1,0:T(8,128)S(1)}, u32[]{:S(2)}, u32[]{:S(2)}) collective-permute-start(f32[24,4096]{1,0:T(8,128)S(1)} %add.163), channel_id=1, source_target_pairs={{0,4},{1,5},{2,6},{3,7},{4,0},{5,1},{6,2},{7,3},{8,12},{9,13},{10,... | collective-permute-start | bytes 1179656 | tf_op jit(solution)/shard_map/ppermute | solution.py:189
  252.6 17.9 %collective-permute-done.2 = f32[24,4096]{1,0:T(8,128)S(1)} collective-permute-done((f32[24,4096]{1,0:T(8,128)S(1)}, f32[24,4096]{1,0:T(8,128)S(1)}, u32[]{:S(2)}, u32[]{:S(2)}) %collective-permute-start.2) | collective-permute-done | bytes 393248 | tf_op jit(solution)/shard_map/ppermute | solution.py:189
  (206 shorter events, 41.0 us)
Async XLA Ops:
  7.2 202.7 %copy-start = (bf16[24,128,128]{2,1,0:T(8,128)(2,1)S(1)}, bf16[24,128,128]{2,1,0:T(8,128)(2,1)}, u32[]{:S(2)}) copy-start(bf16[24,128,128]{2,1,0:T(8,128)(2,1)} %param.20) | copy-start | bytes 2359300
  7.2 203.6 %reduce-scatter.3.cloned.1.call-start = ((), (), s32[]{:S(2)}) async-start(), calls=%async_computation.1 | async-start | bytes 1622016 | tf_op jit(solution)/shard_map/reduce_scatter | solution.py:139
  84.6 2.4 copy-start.2
  84.6 3.2 %copy-start.7 = (u32[256]{0:T(256)S(1)}, u32[256]{0:T(256)}, u32[]{:S(2)}) copy-start(u32[256]{0:T(256)} %constant.130) | copy-start | bytes 3076
  84.6 125.0 %copy-start.4 = (bf16[24,128]{1,0:T(8,128)(2,1)S(1)}, bf16[24,128]{1,0:T(8,128)(2,1)}, u32[]{:S(2)}) copy-start(bf16[24,128]{1,0:T(8,128)(2,1)} %param.17) | copy-start | bytes 18436
  84.6 125.1 %copy-start.6 = (bf16[24,128]{1,0:T(8,128)(2,1)S(1)}, bf16[24,128]{1,0:T(8,128)(2,1)}, u32[]{:S(2)}) copy-start(bf16[24,128]{1,0:T(8,128)(2,1)} %param.16) | copy-start | bytes 18436
  84.6 127.0 %copy-start.5 = (bf16[24,128,128]{2,1,0:T(8,128)(2,1)S(1)}, bf16[24,128,128]{2,1,0:T(8,128)(2,1)}, u32[]{:S(2)}) copy-start(bf16[24,128,128]{2,1,0:T(8,128)(2,1)} %param.21) | copy-start | bytes 2359300
  212.0 40.6 %copy-start.3 = (bf16[4096]{0:T(1024)(128)(2,1)S(1)}, bf16[4096]{0:T(1024)(128)(2,1)}, u32[]{:S(2)}) copy-start(bf16[4096]{0:T(1024)(128)(2,1)} %param.27) | copy-start | bytes 24580
  212.0 58.5 %copy-start.1 = (bf16[24,4096]{1,0:T(8,128)(2,1)S(1)}, bf16[24,4096]{1,0:T(8,128)(2,1)}, u32[]{:S(2)}) copy-start(bf16[24,4096]{1,0:T(8,128)(2,1)} %param.26) | copy-start | bytes 589828
  214.9 9.4 %collective-permute-start = (f32[24,4096]{1,0:T(8,128)S(1)}, f32[24,4096]{1,0:T(8,128)S(1)}, u32[]{:S(2)}, u32[]{:S(2)}) collective-permute-start(f32[24,4096]{1,0:T(8,128)S(1)} %fusion.36), channel_id=1, source_target_pairs={{0,1},{1,0},{2,3},{3,2},{4,5},{5,4},{6,7},{7,6},{8,9},{9,8},{10,11... | collective-permute-start | bytes 1179656 | tf_op jit(solution)/shard_map/ppermute | solution.py:189
  224.4 20.4 %collective-permute-start.1 = (f32[24,4096]{1,0:T(8,128)S(1)}, f32[24,4096]{1,0:T(8,128)S(1)}, u32[]{:S(2)}, u32[]{:S(2)}) collective-permute-start(f32[24,4096]{1,0:T(8,128)S(1)} %add.162), channel_id=1, source_target_pairs={{0,2},{1,3},{2,0},{3,1},{4,6},{5,7},{6,4},{7,5},{8,10},{9,11},{10,... | collective-permute-start | bytes 1179656 | tf_op jit(solution)/shard_map/ppermute | solution.py:189
  244.8 25.7 %collective-permute-start.2 = (f32[24,4096]{1,0:T(8,128)S(1)}, f32[24,4096]{1,0:T(8,128)S(1)}, u32[]{:S(2)}, u32[]{:S(2)}) collective-permute-start(f32[24,4096]{1,0:T(8,128)S(1)} %add.163), channel_id=1, source_target_pairs={{0,4},{1,5},{2,6},{3,7},{4,0},{5,1},{6,2},{7,3},{8,12},{9,13},{10,... | collective-permute-start | bytes 1179656 | tf_op jit(solution)/shard_map/ppermute | solution.py:189
Sparse Core Ops, SparseCore 0:
  87.1 86.9 reduce-scatter.2
